TPU v7x, 512 devices: a whole 4x8x8 slice. The times are simulated.
512 devices in a mesh: pipe: 4 (over z_hi), ctx: 32 (over y, z_lo, core), dp: 4 (over x).
Axes of the slice: x: 4, y: 8, z: 8 (z_hi: 4, z_lo: 2; z = z_hi * 2 + z_lo), core: 2. Of those that a mesh axis runs over, the one named last changes fastest.
Arguments:
- queries: bfloat16 [4, 4, 4096, 4096], P('pipe', 'dp', 'ctx'), may hold values from -7 to 7
- key_input: bfloat16 [4, 4, 4096, 512], P('pipe', 'dp', 'ctx'), may hold values from -4 to 4
- value_input: bfloat16 [4, 4, 4096, 512], P('pipe', 'dp', 'ctx'), may hold values from -6 to 6
- incoming: bfloat16 [4, 4, 4096, 4096], P('pipe', 'dp', 'ctx'), may hold values from -6 to 6
- segments: int32 [4, 4096], P('dp'), may hold values from 0 to 15, never falling along the last dimension, each value on 1 to 512 neighbouring positions
Outputs:
- query_grad: bfloat16 [4, 4, 4096, 4096], P('pipe', 'dp', 'ctx')
- key_grad: bfloat16 [4, 4, 4096, 512], P('pipe', 'dp', 'ctx')
- value_grad: bfloat16 [4, 4, 4096, 512], P('pipe', 'dp', 'ctx')
- bias_grad: float32 [4, 5120], P('pipe')
Inputs may be any that keep to these rules, and one draw needn't show every extreme that they name: `segments`: tokens of one document are contiguous; every document holds 1 to 512 tokens and one holds exactly 512.
All inputs are finite; a program needn't handle non-finite values.
Results may differ from a plain program's by a relative error of at most 0.009.
Values may be sent and summed in bfloat16 or wider, within the bound.
No kernel may reach another device: no remote copies, remote signals or barrier semaphores. Data moves between devices by JAX's collectives and lax.ppermute only.
A program may use at most 64 MiB of HBM per device.

v0:
```python
import math
import jax
import jax.numpy as jnp
from jax import lax
from jax.sharding import PartitionSpec as P

ASKER_STREAMS = 32
SHARED_GROUPS = 4
FEATURE_SIZE = 128
QUERY_PER_KEY = 8


def passed_along(value, axis, steps):
    count = lax.axis_size(axis)
    pairs = [(source, (source + steps) % count) for source in range(count)]
    return lax.ppermute(value, axis, pairs)


def attend(
    queries, key_rows, value_rows, cotangent, query_doc, key_doc, query_pos, key_pos, scaling
):
    scores = (
        jnp.einsum("gqd,kd->gqk", queries, key_rows, preferred_element_type=jnp.float32) * scaling
    )
    visible = (query_doc[:, None] == key_doc[None, :]) & (key_pos[None, :] <= query_pos[:, None])
    scores = jnp.where(visible[None], scores, -1e30)
    row_max = jnp.max(scores, axis=-1, keepdims=True)
    weights = jnp.where(visible[None], jnp.exp(scores - row_max), 0.0)
    probs = weights / jnp.sum(weights, axis=-1, keepdims=True)
    probs_b = probs.astype(jnp.bfloat16)
    attn_out = jnp.einsum("gqk,kd->gqd", probs_b, value_rows, preferred_element_type=jnp.float32)
    dot_out = jnp.sum(cotangent.astype(jnp.float32) * attn_out, axis=-1, keepdims=True)
    grad_prob = jnp.einsum("gqd,kd->gqk", cotangent, value_rows, preferred_element_type=jnp.float32)
    grad_score = (probs * (grad_prob - dot_out) * scaling).astype(jnp.bfloat16)
    asker_derivative = jnp.einsum(
        "gqk,kd->gqd", grad_score, key_rows, preferred_element_type=jnp.float32
    )
    lookup_derivative = jnp.einsum(
        "gqk,gqd->kd", grad_score, queries, preferred_element_type=jnp.float32
    )
    content_derivative = jnp.einsum(
        "gqk,gqd->kd", probs_b, cotangent, preferred_element_type=jnp.float32
    )
    return (asker_derivative, lookup_derivative, content_derivative)


def banded(queries, key_rows, value_rows, cotangent, doc_ids, block_len, scaling):
    length = doc_ids.shape[0]
    blocks = length // block_len
    width = key_rows.shape[1]
    key_pad = jnp.concatenate([jnp.zeros((block_len, width), key_rows.dtype), key_rows], axis=0)
    value_pad = jnp.concatenate(
        [jnp.zeros((block_len, width), value_rows.dtype), value_rows], axis=0
    )
    doc_pad = jnp.concatenate([jnp.full((block_len,), -1, jnp.int32), doc_ids])
    pos_pad = jnp.arange(length + block_len, dtype=jnp.int32) - block_len

    def step(carried, block):
        key_acc, value_acc = carried
        anchor = block * block_len
        query_blk = lax.dynamic_slice_in_dim(queries, anchor, block_len, 1)
        cot_blk = lax.dynamic_slice_in_dim(cotangent, anchor, block_len, 1)
        key_blk = lax.dynamic_slice_in_dim(key_pad, anchor, 2 * block_len, 0)
        value_blk = lax.dynamic_slice_in_dim(value_pad, anchor, 2 * block_len, 0)
        query_doc = lax.dynamic_slice_in_dim(doc_ids, anchor, block_len, 0)
        key_doc = lax.dynamic_slice_in_dim(doc_pad, anchor, 2 * block_len, 0)
        query_pos = anchor + jnp.arange(block_len, dtype=jnp.int32)
        key_pos = lax.dynamic_slice_in_dim(pos_pad, anchor, 2 * block_len, 0)
        asker_derivative, lookup_derivative, content_derivative = attend(
            query_blk, key_blk, value_blk, cot_blk, query_doc, key_doc, query_pos, key_pos, scaling
        )
        key_acc = lax.dynamic_update_slice_in_dim(
            key_acc,
            lax.dynamic_slice_in_dim(key_acc, anchor, 2 * block_len, 0) + lookup_derivative,
            anchor,
            0,
        )
        value_acc = lax.dynamic_update_slice_in_dim(
            value_acc,
            lax.dynamic_slice_in_dim(value_acc, anchor, 2 * block_len, 0) + content_derivative,
            anchor,
            0,
        )
        return ((key_acc, value_acc), asker_derivative)

    start_acc = jnp.zeros((length + block_len, width), jnp.float32)
    (key_acc, value_acc), query_blocks = lax.scan(
        step, (start_acc, start_acc), jnp.arange(blocks, dtype=jnp.int32)
    )
    groups = queries.shape[0]
    asker_derivative = query_blocks.transpose(1, 0, 2, 3).reshape(groups, length, width)
    return (asker_derivative, key_acc[block_len:], value_acc[block_len:])


def body(queries, key_input, value_input, incoming, segments):
    shard_length = queries.shape[2]
    ctx_size = lax.axis_size("ctx")
    reach_dev = min(4, ctx_size - 1)
    block_len = reach_dev * shard_length
    scaling = 1.0 / math.sqrt(FEATURE_SIZE)
    doc_ids = segments[0]
    handed = passed_along(incoming, "pipe", -1)
    query_tok = queries[0, 0].reshape(shard_length, ASKER_STREAMS, FEATURE_SIZE)
    cot_tok = handed[0, 0].reshape(shard_length, ASKER_STREAMS, FEATURE_SIZE)
    key_widened = jnp.repeat(
        key_input[0, 0].reshape(shard_length, SHARED_GROUPS, FEATURE_SIZE), QUERY_PER_KEY, axis=1
    )
    value_widened = jnp.repeat(
        value_input[0, 0].reshape(shard_length, SHARED_GROUPS, FEATURE_SIZE), QUERY_PER_KEY, axis=1
    )
    query_head, key_head, value_head, cot_head = (
        lax.all_to_all(query_tok, "ctx", split_axis=1, concat_axis=0, tiled=True),
        lax.all_to_all(key_widened, "ctx", split_axis=1, concat_axis=0, tiled=True),
        lax.all_to_all(value_widened, "ctx", split_axis=1, concat_axis=0, tiled=True),
        lax.all_to_all(cot_tok, "ctx", split_axis=1, concat_axis=0, tiled=True),
    )

    def per_head(members):
        return banded(
            members[0][None], members[1], members[2], members[3][None], doc_ids, block_len, scaling
        )

    asker_derivative, lookup_derivative, content_derivative = lax.map(
        per_head,
        (
            query_head.transpose(1, 0, 2),
            key_head.transpose(1, 0, 2),
            value_head.transpose(1, 0, 2),
            cot_head.transpose(1, 0, 2),
        ),
    )
    asker_derivative = asker_derivative[:, 0].transpose(1, 0, 2)
    lookup_derivative = lookup_derivative.transpose(1, 0, 2)
    content_derivative = content_derivative.transpose(1, 0, 2)
    query_back, key_backward, value_backward = (
        lax.all_to_all(asker_derivative, "ctx", split_axis=0, concat_axis=1, tiled=True),
        lax.all_to_all(lookup_derivative, "ctx", split_axis=0, concat_axis=1, tiled=True),
        lax.all_to_all(content_derivative, "ctx", split_axis=0, concat_axis=1, tiled=True),
    )
    query_flat = query_back.reshape(shard_length, ASKER_STREAMS * FEATURE_SIZE)
    key_flattened = (
        key_backward.reshape(shard_length, SHARED_GROUPS, QUERY_PER_KEY, FEATURE_SIZE)
        .sum(axis=2)
        .reshape(shard_length, SHARED_GROUPS * FEATURE_SIZE)
    )
    value_flat = (
        value_backward.reshape(shard_length, SHARED_GROUPS, QUERY_PER_KEY, FEATURE_SIZE)
        .sum(axis=2)
        .reshape(shard_length, SHARED_GROUPS * FEATURE_SIZE)
    )
    offset_parts = jnp.concatenate(
        [jnp.sum(query_flat, axis=0), jnp.sum(key_flattened, axis=0), jnp.sum(value_flat, axis=0)]
    )
    pipe_idx = lax.axis_index("pipe")
    slots = (
        jnp.zeros((lax.axis_size("pipe"), offset_parts.shape[0]), jnp.float32)
        .at[pipe_idx]
        .set(offset_parts)
    )
    offset_overall = lax.psum(slots, ("pipe", "ctx", "dp"))[pipe_idx]
    bias_scaled = offset_overall / math.sqrt(lax.axis_size("dp") * shard_length * ctx_size)
    query_grad = query_flat.astype(jnp.bfloat16)[None, None]
    key_grad = key_flattened.astype(jnp.bfloat16)[None, None]
    value_grad = value_flat.astype(jnp.bfloat16)[None, None]
    return (query_grad, key_grad, value_grad, bias_scaled[None])


def solution(mesh):
    return jax.shard_map(
        body,
        mesh=mesh,
        in_specs=(
            P("pipe", "dp", "ctx", None),
            P("pipe", "dp", "ctx", None),
            P("pipe", "dp", "ctx", None),
            P("pipe", "dp", "ctx", None),
            P("dp", None),
        ),
        out_specs=(
            P("pipe", "dp", "ctx", None),
            P("pipe", "dp", "ctx", None),
            P("pipe", "dp", "ctx", None),
            P("pipe", None),
        ),
        check_vma=False,
    )
```

profile of v0, /device:TPU:1, one launch (start us, length us, event | category | flops | bytes accessed | tf_op | source)
XLA Modules:
  0.0 760.0 jit_solution(13099326957965084261)
XLA Ops:
  9.4 10.6 %all-to-all-start.1 = ((bf16[128,32,128]{2,0,1:T(8,128)(2,1)}), bf16[128,32,128]{2,0,1:T(8,128)(2,1)S(1)}, u32[]{:S(2)}, u32[]{:S(2)}) async-start(bf16[128,32,128]{2,0,1:T(8,128)(2,1)} %bitcast.9), calls=%async_computation.1 | async-start | bytes 2097152 | tf_op jit(solution)/shard_map/all_to_all | solution.py:113
  20.0 28.0 %all-to-all-done.1 = bf16[128,32,128]{2,0,1:T(8,128)(2,1)S(1)} async-done(((bf16[128,32,128]{2,0,1:T(8,128)(2,1)}), bf16[128,32,128]{2,0,1:T(8,128)(2,1)S(1)}, u32[]{:S(2)}, u32[]{:S(2)}) %all-to-all-start.1) | async-done | bytes 1048608 | tf_op jit(solution)/shard_map/all_to_all | solution.py:113
  49.2 4.3 all-to-all-start.3
  53.6 9.8 %collective-permute-start = (bf16[1,1,128,4096]{3,2,1,0:T(8,128)(2,1)}, bf16[1,1,128,4096]{3,2,1,0:T(8,128)(2,1)S(1)}, u32[]{:S(2)}, u32[]{:S(2)}) collective-permute-start(bf16[1,1,128,4096]{3,2,1,0:T(8,128)(2,1)} %param.12), channel_id=1, source_target_pairs={{0,384},{128,0},{256,128},{384,256},{1,385},{129,1},{257,129},{385... | collective-permute-start | bytes 3145736 | tf_op jit(solution)/shard_map/ppermute | solution.py:16
  63.3 54.2 %collective-permute-done = bf16[1,1,128,4096]{3,2,1,0:T(8,128)(2,1)S(1)} collective-permute-done((bf16[1,1,128,4096]{3,2,1,0:T(8,128)(2,1)}, bf16[1,1,128,4096]{3,2,1,0:T(8,128)(2,1)S(1)}, u32[]{:S(2)}, u32[]{:S(2)}) %collective-permute-start) | collective-permute-done | bytes 1048608 | tf_op jit(solution)/shard_map/ppermute | solution.py:16
  118.9 6.5 all-to-all-start.2
  128.2 25.2 %all-to-all-done.2 = bf16[128,32,128]{0,2,1:T(8,128)(2,1)S(1)} async-done(((bf16[128,32,128]{0,2,1:T(8,128)(2,1)}), bf16[128,32,128]{0,2,1:T(8,128)(2,1)S(1)}, u32[]{:S(2)}, u32[]{:S(2)}) %all-to-all-start.2) | async-done | bytes 1048608 | tf_op jit(solution)/shard_map/all_to_all | solution.py:115
  153.5 5.0 all-to-all-start
  162.2 24.3 %all-to-all-done = bf16[128,32,128]{2,0,1:T(8,128)(2,1)} async-done(((bf16[128,32,128]{2,0,1:T(8,128)(2,1)}), bf16[128,32,128]{2,0,1:T(8,128)(2,1)}, u32[]{:S(2)}, u32[]{:S(2)}) %all-to-all-start) | async-done | bytes 1048608 | tf_op jit(solution)/shard_map/all_to_all | solution.py:112
  190.1 126.4 %while.26 = (s32[]{:T(128)}, f32[4608,128]{1,0:T(8,128)}, f32[4608,128]{1,0:T(8,128)}, f32[8,1,512,128]{3,2,1,0:T(8,128)}, s32[8]{0:T(128)}, /*index=5*/s32[4096...) while((s32[]{:T(128)}, f32[4608,128]{1,0:T(8,128)}, ...), condition=%wide.region_4.5_spmd, body=%wide.region_0.4_spmd.sunk | while | flops 820444160 | bytes 22487344 | solution.py:87
  199.1 2.4 fusion.59
  201.5 2.3 fusion.60
  214.9 2.4 fusion.59
  217.3 2.3 fusion.60
  230.7 2.4 fusion.59
  233.1 2.3 fusion.60
  246.5 2.4 fusion.59
  262.3 2.4 fusion.59
  264.7 2.3 fusion.60
  278.1 2.4 fusion.59
  280.5 2.3 fusion.60
  293.9 2.4 fusion.59
  296.3 2.3 fusion.60
  309.7 2.4 fusion.59
  312.1 2.3 fusion.60
  316.5 3.1 slice.22
  319.7 6.0 all-to-all-start.5
  327.1 48.6 %all-to-all-done.5 = f32[4096,1,128]{2,1,0:T(1,128)} async-done(((f32[4096,1,128]{2,1,0:T(1,128)}), f32[4096,1,128]{2,1,0:T(1,128)}, u32[]{:S(2)}, u32[]{:S(2)}) %all-to-all-start.5) | async-done | bytes 2097184 | tf_op jit(solution)/shard_map/all_to_all | solution.py:137
  375.7 56.1 %all_to_all.105 = f32[4096,1,128]{2,1,0:T(1,128)S(1)} all-to-all(f32[4096,1,128]{2,1,0:T(1,128)} %bitcast.107), channel_id=1, replica_groups=mesh['pipe'=4,'ctx'=32,'dp'=4] {'ctx'}, dimensions={0} | all-to-all | bytes 4194304 | tf_op jit(solution)/shard_map/all_to_all | solution.py:138
  431.9 6.0 all-to-all-start.4
  440.6 47.4 %all-to-all-done.4 = f32[4096,1,128]{2,1,0:T(1,128)} async-done(((f32[4096,1,128]{2,1,0:T(1,128)}), f32[4096,1,128]{2,1,0:T(1,128)}, u32[]{:S(2)}, u32[]{:S(2)}) %all-to-all-start.4) | async-done | bytes 2097184 | tf_op jit(solution)/shard_map/all_to_all | solution.py:136
  500.4 251.3 %all-reduce.5.cloned.1.call-done = f32[4,5120]{1,0:T(4,128)} async-done(((f32[4,5120]{1,0:T(4,128)}), f32[4,5120]{1,0:T(4,128)}) %all-reduce.5.cloned.1.call-update) | async-done | bytes 81936 | tf_op jit(solution)/shard_map/psum | solution.py:160
  (156 shorter events, 119.1 us)
Async XLA Ops:
  7.2 12.8 %copy-start.2 = (bf16[1,1,128,512]{3,2,1,0:T(8,128)(2,1)S(1)}, bf16[1,1,128,512]{3,2,1,0:T(8,128)(2,1)}, u32[]{:S(2)}) copy-start(bf16[1,1,128,512]{3,2,1,0:T(8,128)(2,1)} %param.11) | copy-start | bytes 393220
  9.4 38.6 %all-to-all-start.1 = ((bf16[128,32,128]{2,0,1:T(8,128)(2,1)}), bf16[128,32,128]{2,0,1:T(8,128)(2,1)S(1)}, u32[]{:S(2)}, u32[]{:S(2)}) async-start(bf16[128,32,128]{2,0,1:T(8,128)(2,1)} %bitcast.9), calls=%async_computation.1 | async-start | bytes 2097152 | tf_op jit(solution)/shard_map/all_to_all | solution.py:113
  49.2 69.6 %all-to-all-start.3 = ((bf16[128,32,128]{2,0,1:T(8,128)(2,1)}), bf16[128,32,128]{2,0,1:T(8,128)(2,1)S(1)}, u32[]{:S(2)}, u32[]{:S(2)}) async-start(bf16[128,32,128]{2,0,1:T(8,128)(2,1)} %bitcast.17), calls=%async_computation.3 | async-start | bytes 2097152 | tf_op jit(solution)/shard_map/all_to_all | solution.py:114
  53.6 64.0 %collective-permute-start = (bf16[1,1,128,4096]{3,2,1,0:T(8,128)(2,1)}, bf16[1,1,128,4096]{3,2,1,0:T(8,128)(2,1)S(1)}, u32[]{:S(2)}, u32[]{:S(2)}) collective-permute-start(bf16[1,1,128,4096]{3,2,1,0:T(8,128)(2,1)} %param.12), channel_id=1, source_target_pairs={{0,384},{128,0},{256,128},{384,256},{1,385},{129,1},{257,129},{385... | collective-permute-start | bytes 3145736 | tf_op jit(solution)/shard_map/ppermute | solution.py:16
  118.9 34.6 %all-to-all-start.2 = ((bf16[128,32,128]{0,2,1:T(8,128)(2,1)}), bf16[128,32,128]{0,2,1:T(8,128)(2,1)S(1)}, u32[]{:S(2)}, u32[]{:S(2)}) async-start(bf16[128,32,128]{0,2,1:T(8,128)(2,1)} %bitcast.110), calls=%async_computation.2 | async-start | bytes 2097152 | tf_op jit(solution)/shard_map/all_to_all | solution.py:115
  126.8 31.6 %copy-start.3 = (s32[1,4096]{1,0:T(1,128)S(1)}, s32[1,4096]{1,0:T(1,128)}, u32[]{:S(2)}) copy-start(s32[1,4096]{1,0:T(1,128)} %param.13) | copy-start | bytes 49156
  153.5 33.0 %all-to-all-start = ((bf16[128,32,128]{2,0,1:T(8,128)(2,1)}), bf16[128,32,128]{2,0,1:T(8,128)(2,1)}, u32[]{:S(2)}, u32[]{:S(2)}) async-start(bf16[128,32,128]{2,0,1:T(8,128)(2,1)} %copy.41), calls=%async_computation | async-start | bytes 2097152 | tf_op jit(solution)/shard_map/all_to_all | solution.py:112
  319.7 6.0 copy-start
  319.7 56.1 %all-to-all-start.5 = ((f32[4096,1,128]{2,1,0:T(1,128)}), f32[4096,1,128]{2,1,0:T(1,128)}, u32[]{:S(2)}, u32[]{:S(2)}) async-start(f32[4096,1,128]{2,1,0:T(1,128)} %bitcast.106), calls=%async_computation.5 | async-start | bytes 4194304 | tf_op jit(solution)/shard_map/all_to_all | solution.py:137
  431.9 6.1 copy-start.4
  431.9 56.1 %all-to-all-start.4 = ((f32[4096,1,128]{2,1,0:T(1,128)}), f32[4096,1,128]{2,1,0:T(1,128)}, u32[]{:S(2)}, u32[]{:S(2)}) async-start(f32[4096,1,128]{2,1,0:T(1,128)} %bitcast.114), calls=%async_computation.4 | async-start | bytes 4194304 | tf_op jit(solution)/shard_map/all_to_all | solution.py:136
  437.9 313.8 %all-reduce.5.cloned.1.call-start = ((), (), s32[]{:S(2)}) async-start(), calls=%async_computation.7 | async-start | bytes 163840 | tf_op jit(solution)/shard_map/psum | solution.py:160
  490.7 0.6 copy-start.1
Sparse Core Ops, SparseCore 0:
  491.5 260.1 all-reduce.4
where the time goes:
time: 763 us; the launch traced here: 760 us
  waiting for transfers between devices  479 us (63%)
  matrix products  76.2 us (10%)
  local copies, waits for them, and re-layouts  56.1 us (7%)
  blocking collectives  56.1 us (7%)
  starting transfers between devices  48.2 us (6%)
  other arithmetic  25.3 us (3%)
  between operations  14.3 us (2%)
    psum x1, waiting for transfers between devices, body(): offset_overall = lax.psum(slots, ('pipe', 'ctx', 'dp'))[pipe_idx]  251 us
    all_to_all x1, blocking collectives, body(): lax.all_to_all(content_derivative, 'ctx', split_axis=0, concat_axis=1, ti...  56.1 us
    ppermute x1, waiting for transfers between devices, passed_along(): return lax.ppermute(value, axis, pairs)  54.2 us
    all_to_all x1, waiting for transfers between devices, body(): lax.all_to_all(lookup_derivative, 'ctx', split_axis=0, concat_axis=1, til...  48.6 us
    all_to_all x1, waiting for transfers between devices, body(): lax.all_to_all(asker_derivative, 'ctx', split_axis=0, concat_axis=1, tile...  47.4 us
    all_to_all x1, waiting for transfers between devices, body(): lax.all_to_all(key_widened, 'ctx', split_axis=1, concat_axis=0, tiled=True)  28 us
    all_to_all x1, waiting for transfers between devices, body(): lax.all_to_all(cot_tok, 'ctx', split_axis=1, concat_axis=0, tiled=True)  25.2 us
    all_to_all x1, waiting for transfers between devices, body(): lax.all_to_all(query_tok, 'ctx', split_axis=1, concat_axis=0, tiled=True)  24.3 us
  transfers between devices with their start and end apart: 8, of which 7 were waited for; matrix products, arithmetic and copies ran while one was open for 3% of the time, Pallas kernels for 0%

commit v1 on v0

--- a/solution.py
+++ b/solution.py
@@ -157,7 +157,7 @@
         .at[pipe_idx]
         .set(offset_parts)
     )
-    offset_overall = lax.psum(slots, ("pipe", "ctx", "dp"))[pipe_idx]
+    offset_overall = jnp.sum(lax.all_gather(slots, ("pipe", "ctx", "dp")), axis=0)[pipe_idx]
     bias_scaled = offset_overall / math.sqrt(lax.axis_size("dp") * shard_length * ctx_size)
     query_grad = query_flat.astype(jnp.bfloat16)[None, None]
     key_grad = key_flattened.astype(jnp.bfloat16)[None, None]

time: 763 us -> 1990 us (2.61)
  waiting for transfers between devices: 479 us -> 1690 us
    all_gather x0 -> x1, waiting for transfers between devices: none -> 1460 us  [body(): lax.all_gather(slots, ('pipe', 'ctx', 'dp'))]
    psum x1 -> x0, waiting for transfers between devices: 251 us -> none  [body(): offset_overall = lax.psum(slots, ('pipe', 'ctx', 'dp'))[pipe_idx]]
  transfers between devices with their start and end apart: 8 -> 8, of which waited for: 7 -> 7; matrix products, arithmetic and copies ran while one was open for 3% -> 1% of each run, Pallas kernels for 0% -> 0%
where the time goes in v1:
time: 1990 us; the launch traced here: 1980 us
  waiting for transfers between devices  1690 us (85%)
  matrix products  76.2 us (4%)
  local copies, waits for them, and re-layouts  56.2 us (3%)
  blocking collectives  56.1 us (3%)
  starting transfers between devices  48.2 us (2%)
  other arithmetic  38.6 us (2%)
    all_gather x1, waiting for transfers between devices, body(): lax.all_gather(slots, ('pipe', 'ctx', 'dp'))  1460 us
    all_to_all x1, blocking collectives, body(): lax.all_to_all(content_derivative, 'ctx', split_axis=0, concat_axis=1, ti...  56.1 us
    ppermute x1, waiting for transfers between devices, passed_along(): return lax.ppermute(value, axis, pairs)  54.2 us
    all_to_all x1, waiting for transfers between devices, body(): lax.all_to_all(lookup_derivative, 'ctx', split_axis=0, concat_axis=1, til...  48.6 us
    all_to_all x1, waiting for transfers between devices, body(): lax.all_to_all(asker_derivative, 'ctx', split_axis=0, concat_axis=1, tile...  47.4 us
  transfers between devices with their start and end apart: 8, of which 7 were waited for; matrix products, arithmetic and copies ran while one was open for 1% of the time, Pallas kernels for 0%

profile of v1, /device:TPU:1, one launch (start us, length us, event | category | flops | bytes accessed | tf_op | source)
XLA Modules:
  0.0 1981.0 jit_solution(7645943773810092349)
XLA Ops:
  9.4 10.6 all-to-all-start.1
  20.0 28.0 %all-to-all-done.1 = bf16[128,32,128]{2,0,1:T(8,128)(2,1)S(1)} async-done(((bf16[128,32,128]{2,0,1:T(8,128)(2,1)}), bf16[128,32,128]{2,0,1:T(8,128)(2,1)S(1)}, u32[]{:S(2)}, u32[]{:S(2)}) %all-to-all-start.1) | async-done | bytes 1048608 | tf_op jit(solution)/shard_map/all_to_all | solution.py:113
  49.2 4.3 all-to-all-start.3
  53.6 9.8 collective-permute-start
  63.3 54.2 %collective-permute-done = bf16[1,1,128,4096]{3,2,1,0:T(8,128)(2,1)S(1)} collective-permute-done((bf16[1,1,128,4096]{3,2,1,0:T(8,128)(2,1)}, bf16[1,1,128,4096]{3,2,1,0:T(8,128)(2,1)S(1)}, u32[]{:S(2)}, u32[]{:S(2)}) %collective-permute-start) | collective-permute-done | bytes 1048608 | tf_op jit(solution)/shard_map/ppermute | solution.py:16
  118.9 6.5 all-to-all-start.2
  128.2 25.2 %all-to-all-done.2 = bf16[128,32,128]{0,2,1:T(8,128)(2,1)S(1)} async-done(((bf16[128,32,128]{0,2,1:T(8,128)(2,1)}), bf16[128,32,128]{0,2,1:T(8,128)(2,1)S(1)}, u32[]{:S(2)}, u32[]{:S(2)}) %all-to-all-start.2) | async-done | bytes 1048608 | tf_op jit(solution)/shard_map/all_to_all | solution.py:115
  153.5 5.0 all-to-all-start
  162.2 24.3 %all-to-all-done = bf16[128,32,128]{2,0,1:T(8,128)(2,1)} async-done(((bf16[128,32,128]{2,0,1:T(8,128)(2,1)}), bf16[128,32,128]{2,0,1:T(8,128)(2,1)}, u32[]{:S(2)}, u32[]{:S(2)}) %all-to-all-start) | async-done | bytes 1048608 | tf_op jit(solution)/shard_map/all_to_all | solution.py:112
  190.1 126.4 %while.26 = (s32[]{:T(128)}, f32[4608,128]{1,0:T(8,128)}, f32[4608,128]{1,0:T(8,128)}, f32[8,1,512,128]{3,2,1,0:T(8,128)}, s32[8]{0:T(128)}, /*index=5*/s32[4096...) while((s32[]{:T(128)}, f32[4608,128]{1,0:T(8,128)}, ...), condition=%wide.region_4.5_spmd, body=%wide.region_0.4_spmd.sunk | while | flops 820444160 | bytes 22487344 | solution.py:87
  199.1 2.4 fusion.59
  201.5 2.3 fusion.60
  214.9 2.4 fusion.59
  217.3 2.3 fusion.60
  230.7 2.4 fusion.59
  233.1 2.3 fusion.60
  246.5 2.4 fusion.59
  262.3 2.4 fusion.59
  264.7 2.3 fusion.60
  278.1 2.4 fusion.59
  280.5 2.3 fusion.60
  293.9 2.4 fusion.59
  296.3 2.3 fusion.60
  309.7 2.4 fusion.59
  316.5 3.1 slice.22
  319.7 6.0 all-to-all-start.5
  327.2 48.6 %all-to-all-done.5 = f32[4096,1,128]{2,1,0:T(1,128)} async-done(((f32[4096,1,128]{2,1,0:T(1,128)}), f32[4096,1,128]{2,1,0:T(1,128)}, u32[]{:S(2)}, u32[]{:S(2)}) %all-to-all-start.5) | async-done | bytes 2097184 | tf_op jit(solution)/shard_map/all_to_all | solution.py:137
  375.7 56.1 %all_to_all.105 = f32[4096,1,128]{2,1,0:T(1,128)S(1)} all-to-all(f32[4096,1,128]{2,1,0:T(1,128)} %bitcast.107), channel_id=1, replica_groups=mesh['pipe'=4,'ctx'=32,'dp'=4] {'ctx'}, dimensions={0} | all-to-all | bytes 4194304 | tf_op jit(solution)/shard_map/all_to_all | solution.py:138
  431.9 6.0 all-to-all-start.4
  440.6 47.4 %all-to-all-done.4 = f32[4096,1,128]{2,1,0:T(1,128)} async-done(((f32[4096,1,128]{2,1,0:T(1,128)}), f32[4096,1,128]{2,1,0:T(1,128)}, u32[]{:S(2)}, u32[]{:S(2)}) %all-to-all-start.4) | async-done | bytes 2097184 | tf_op jit(solution)/shard_map/all_to_all | solution.py:136
  500.4 1459.1 %all-gather.2.cloned.1.call-done = f32[512,4,5120]{2,1,0:T(4,128)} async-done(((f32[1,4,5120]{2,1,0:T(4,128)}), f32[512,4,5120]{2,1,0:T(4,128)}) %all-gather.2.cloned.1.call-update) | async-done | bytes 41943056 | tf_op jit(solution)/shard_map/all_gather | solution.py:160
  1959.4 14.1 reduce_sum.95
  (157 shorter events, 120.5 us)
Async XLA Ops:
  7.2 12.8 copy-start.2
  9.4 38.6 %all-to-all-start.1 = ((bf16[128,32,128]{2,0,1:T(8,128)(2,1)}), bf16[128,32,128]{2,0,1:T(8,128)(2,1)S(1)}, u32[]{:S(2)}, u32[]{:S(2)}) async-start(bf16[128,32,128]{2,0,1:T(8,128)(2,1)} %bitcast.9), calls=%async_computation.1 | async-start | bytes 2097152 | tf_op jit(solution)/shard_map/all_to_all | solution.py:113
  49.2 69.6 %all-to-all-start.3 = ((bf16[128,32,128]{2,0,1:T(8,128)(2,1)}), bf16[128,32,128]{2,0,1:T(8,128)(2,1)S(1)}, u32[]{:S(2)}, u32[]{:S(2)}) async-start(bf16[128,32,128]{2,0,1:T(8,128)(2,1)} %bitcast.17), calls=%async_computation.3 | async-start | bytes 2097152 | tf_op jit(solution)/shard_map/all_to_all | solution.py:114
  53.6 64.0 %collective-permute-start = (bf16[1,1,128,4096]{3,2,1,0:T(8,128)(2,1)}, bf16[1,1,128,4096]{3,2,1,0:T(8,128)(2,1)S(1)}, u32[]{:S(2)}, u32[]{:S(2)}) collective-permute-start(bf16[1,1,128,4096]{3,2,1,0:T(8,128)(2,1)} %param.12), channel_id=1, source_target_pairs={{0,384},{128,0},{256,128},{384,256},{1,385},{129,1},{257,129},{385... | collective-permute-start | bytes 3145736 | tf_op jit(solution)/shard_map/ppermute | solution.py:16
  118.9 34.6 %all-to-all-start.2 = ((bf16[128,32,128]{0,2,1:T(8,128)(2,1)}), bf16[128,32,128]{0,2,1:T(8,128)(2,1)S(1)}, u32[]{:S(2)}, u32[]{:S(2)}) async-start(bf16[128,32,128]{0,2,1:T(8,128)(2,1)} %bitcast.110), calls=%async_computation.2 | async-start | bytes 2097152 | tf_op jit(solution)/shard_map/all_to_all | solution.py:115
  126.8 31.6 %copy-start.3 = (s32[1,4096]{1,0:T(1,128)S(1)}, s32[1,4096]{1,0:T(1,128)}, u32[]{:S(2)}) copy-start(s32[1,4096]{1,0:T(1,128)} %param.13) | copy-start | bytes 49156
  153.5 33.0 %all-to-all-start = ((bf16[128,32,128]{2,0,1:T(8,128)(2,1)}), bf16[128,32,128]{2,0,1:T(8,128)(2,1)}, u32[]{:S(2)}, u32[]{:S(2)}) async-start(bf16[128,32,128]{2,0,1:T(8,128)(2,1)} %copy.41), calls=%async_computation | async-start | bytes 2097152 | tf_op jit(solution)/shard_map/all_to_all | solution.py:112
  319.7 6.0 copy-start
  319.7 56.1 %all-to-all-start.5 = ((f32[4096,1,128]{2,1,0:T(1,128)}), f32[4096,1,128]{2,1,0:T(1,128)}, u32[]{:S(2)}, u32[]{:S(2)}) async-start(f32[4096,1,128]{2,1,0:T(1,128)} %bitcast.106), calls=%async_computation.5 | async-start | bytes 4194304 | tf_op jit(solution)/shard_map/all_to_all | solution.py:137
  431.9 6.1 copy-start.4
  431.9 56.1 %all-to-all-start.4 = ((f32[4096,1,128]{2,1,0:T(1,128)}), f32[4096,1,128]{2,1,0:T(1,128)}, u32[]{:S(2)}, u32[]{:S(2)}) async-start(f32[4096,1,128]{2,1,0:T(1,128)} %bitcast.114), calls=%async_computation.4 | async-start | bytes 4194304 | tf_op jit(solution)/shard_map/all_to_all | solution.py:136
  437.9 1521.5 %all-gather.2.cloned.1.call-start = ((), (), s32[]{:S(2)}) async-start(), calls=%async_computation.7 | async-start | bytes 42024960 | tf_op jit(solution)/shard_map/all_gather | solution.py:160
  490.7 0.6 copy-start.1
Sparse Core Ops, SparseCore 0:
  491.5 1467.8 all-gather.1
